TPU v7x, 512 devices: a whole 4x4x16 slice. The times are simulated.
512 devices in a mesh: smp: 16 (over z), par: 32 (over x, y, core).
Axes of the slice: x: 4, y: 4, z: 16, core: 2. Of those that a mesh axis runs over, the one named last changes fastest.
Arguments:
- jacobian: bfloat16 [4096, 16384], P('smp', 'par'), may hold values from -52 to 52
Outputs:
- panel_factor: float32 [4096, 512], P('smp')
- schur_part: float32 [4096, 4096], P('smp', 'par')
All inputs are finite; a program needn't handle non-finite values.
Results may differ from a plain program's by a relative error of at most 0.0022.
Values may be sent and summed in bfloat16 or wider, within the bound.
No kernel may reach another device: no remote copies, remote signals or barrier semaphores. Data moves between devices by JAX's collectives and lax.ppermute only.
A program may use at most 64 MiB of HBM per device.

v0:
```python
import jax
import jax.numpy as jnp
from jax import lax
from jax.sharding import PartitionSpec as P

PANEL = 512
shift_scale = 0.01


def shards(jacobian):
    row_count, par_width = jacobian.shape
    par_count = lax.axis_size("par")
    smp_count = lax.axis_size("smp")
    sample_total = row_count * smp_count
    param_total = par_width * par_count
    col_width = sample_total // par_count
    panel_piece = PANEL // par_count
    row_index = lax.axis_index("smp")
    col_index = lax.axis_index("par")
    f32 = jnp.float32
    gathered = lax.all_gather(jacobian, "smp", axis=0, tiled=True)
    widened = gathered.astype(f32)
    col_mean = jnp.sum(widened, axis=0) / sample_total
    centered = (widened - col_mean).astype(jnp.bfloat16)
    mine = lax.dynamic_slice_in_dim(centered, row_index * row_count, row_count, 0)
    head = centered[:PANEL]
    contract = (((1,), (1,)), ((), ()))
    main = lax.dot_general(centered, mine, contract, preferred_element_type=f32)
    square = lax.dot_general(head, head, contract, preferred_element_type=f32)
    band = lax.dot_general(centered, head, contract, preferred_element_type=f32)
    sq = centered.astype(f32)
    sumsq = jnp.sum(sq * sq)
    width = row_count
    panel_parts = jnp.concatenate(
        [
            main[:PANEL].reshape(par_count, panel_piece, width),
            square.reshape(par_count, panel_piece * PANEL // width, width),
            jnp.broadcast_to(sumsq, (par_count, 8, width)),
        ],
        axis=1,
    )
    chunk = panel_parts.shape[1]
    reduced = (
        lax.psum_scatter(
            panel_parts.reshape(par_count * chunk, width), "par", scatter_dimension=0, tiled=True
        )
        / param_total
    )
    shared = lax.all_gather(reduced, "par", axis=0, tiled=False)
    main_parts = jnp.concatenate(
        [
            main.reshape(par_count, col_width, width),
            band.reshape(par_count, col_width * PANEL // width, width),
        ],
        axis=1,
    )
    main_parts, shared = lax.optimization_barrier((main_parts, shared))
    main_chunk = main_parts.shape[1]
    reduced_main = (
        lax.psum_scatter(
            main_parts.reshape(par_count * main_chunk, width),
            "par",
            scatter_dimension=0,
            tiled=True,
        )
        / param_total
    )
    tile = reduced_main[:col_width].T
    band_mine = reduced_main[col_width:].reshape(col_width, PANEL)
    o2 = panel_piece
    o3 = o2 + panel_piece * PANEL // width
    panel_t = shared[:, :o2].reshape(PANEL, width)
    square_g = shared[:, o2:o3].reshape(PANEL, PANEL)
    trace_total = shared[0, o3, 0]
    shift_value = shift_scale * trace_total / sample_total
    eye = jnp.arange(PANEL, dtype=jnp.int32)
    global_rows = row_index * row_count + jnp.arange(row_count, dtype=jnp.int32)
    global_cols = col_index * col_width + jnp.arange(col_width, dtype=jnp.int32)
    square_s = square_g + jnp.where(eye[:, None] == eye[None, :], shift_value, 0.0)
    panel_s = panel_t.T + jnp.where(global_rows[:, None] == eye[None, :], shift_value, 0.0)
    band_s = band_mine + jnp.where(global_cols[:, None] == eye[None, :], shift_value, 0.0)
    tile_s = tile + jnp.where(global_rows[:, None] == global_cols[None, :], shift_value, 0.0)
    factor = jnp.linalg.cholesky(square_s)
    panel_out = jax.scipy.linalg.solve_triangular(factor, panel_s.T, lower=True).T
    band_factor = jax.scipy.linalg.solve_triangular(factor, band_s.T, lower=True)
    schur_tile = tile_s - jnp.dot(panel_out, band_factor, precision=lax.Precision.HIGHEST)
    return (panel_out, schur_tile)


def solution(mesh):
    placed = (P("smp", "par"),)
    return jax.shard_map(
        shards,
        mesh=mesh,
        in_specs=placed,
        out_specs=(P("smp", None), P("smp", "par")),
        check_vma=False,
    )
```

profile of v0, /device:TPU:1, one launch (start us, length us, event | category | flops | bytes accessed | tf_op | source)
XLA Modules:
  0.0 437.3 jit_solution(6986741140144333234)
XLA Ops:
  7.2 0.7 all-gather.4.cloned.1.call-update
  7.9 77.4 %all-gather.4.cloned.1.call-done = bf16[4096,512]{1,0:T(8,128)(2,1)} async-done(((bf16[256,512]{1,0:T(8,128)(2,1)}), bf16[4096,512]{1,0:T(8,128)(2,1)}) %all-gather.4.cloned.1.call-update) | async-done | bytes 4194320 | tf_op jit(solution)/shard_map/all_gather | solution.py:21
  85.3 3.0 convert_reduce_fusion
  88.3 0.5 copy-done.2
  88.8 2.8 multiply_reduce_fusion
  91.6 2.0 copy-done
  93.5 0.5 fusion.2
  94.2 3.5 fusion.23
  97.7 1.9 copy-done.1
  99.7 0.6 broadcast_in_dim.46
  100.4 1.5 maximum_maximum_fusion
  102.0 105.5 %reduce-scatter.3.cloned.1.call-done = f32[56,256]{1,0:T(8,128)} async-done(((f32[1792,256]{1,0:T(8,128)}), f32[56,256]{1,0:T(8,128)}) %reduce-scatter.3.cloned.1.call-update) | async-done | bytes 57360 | tf_op jit(solution)/shard_map/reduce_scatter | solution.py:44
  207.5 1.4 broadcast_multiply_fusion.1
  209.0 8.0 %fusion.4 = f32[4096,512]{1,0:T(8,128)} fusion(bf16[4096,512]{1,0:T(8,128)(2,1)} %copy-done), kind=kOutput, calls=%fused_computation.31 | convolution fusion | flops 2147483648 | bytes 13107200 | tf_op jit(solution)/shard_map/dot_general | solution.py:30
  217.0 9.3 %reshape.100 = f32[32,256,256]{2,1,0:T(8,128)} reshape(f32[4096,512]{1,0:T(8,128)} %fusion.4) | data formatting | bytes 16777216 | tf_op jit(solution)/shard_map/reshape | solution.py:53
  226.3 10.5 %pad_maximum_fusion = f32[32,384,256]{2,1,0:T(8,128)} fusion(f32[32,256,256]{2,1,0:T(8,128)} %reshape.100, f32[32,128,256]{2,1,0:T(8,128)} %bitcast.75), kind=kLoop, calls=%fused_computation.2 | loop fusion | flops 3145728 | bytes 25165824 | tf_op jit(solution)/shard_map/concatenate | solution.py:50
  236.8 34.7 %all-gather.6.cloned.1.call-done = f32[1792,256]{1,0:T(8,128)} async-done(((f32[56,256]{1,0:T(8,128)}), f32[1792,256]{1,0:T(8,128)}) %all-gather.6.cloned.1.call-update) | async-done | bytes 1835024 | tf_op jit(solution)/shard_map/all_gather | solution.py:49
  271.5 13.1 %copy.29 = f32[12288,256]{0,1:T(8,128)} copy(f32[12288,256]{1,0:T(8,128)} %bitcast.74) | data formatting | bytes 25165824 | tf_op jit(solution)/shard_map/reshape | solution.py:61
  284.7 1.4 copy-done.4
  286.1 0.5 slice.171
  286.6 0.9 slice.172
  287.6 0.3 reshape.104
  287.9 0.3 copy.14
  289.0 0.3 copy.15
  289.6 11.7 %cholesky.103 = f32[128,128]{1,0:T(8,128)S(1)} custom-call(f32[128,128]{1,0:T(8,128)S(1)} %cholesky.263), custom_call_target="Cholesky" | custom-call | tf_op jit(solution)/shard_map/jit(cholesky)/cholesky | solution.py:83
  301.5 9.8 %custom-call.34 = f32[1,128,128]{1,2,0:T(8,128)S(1)} custom-call(f32[1,128,128]{2,1,0:T(8,128)S(1)} %get-tuple-element.43), custom_call_target="InvertDiagBlocksLowerTriangular" | custom-call | tf_op jit(solution)/shard_map/jit(cholesky)/cholesky | solution.py:83
  311.3 0.3 fusion.26
  311.7 0.3 convolution_subtract_fusion
  312.1 11.7 %cholesky.215 = f32[128,128]{1,0:T(8,128)S(1)} custom-call(f32[128,128]{1,0:T(8,128)S(1)} %cholesky.267), custom_call_target="Cholesky" | custom-call | tf_op jit(solution)/shard_map/jit(cholesky)/cholesky | solution.py:83
  323.9 9.9 %custom-call.35 = f32[1,128,128]{1,2,0:T(8,128)S(1)} custom-call(f32[1,128,128]{2,1,0:T(8,128)S(1)} %get-tuple-element.41), custom_call_target="InvertDiagBlocksLowerTriangular" | custom-call | tf_op jit(solution)/shard_map/jit(cholesky)/cholesky | solution.py:83
  334.1 0.3 convolution_dynamic-update-slice_fusion
  334.4 0.6 convolution_subtract_fusion.4
  335.0 11.7 %cholesky.236 = f32[128,128]{1,0:T(8,128)S(1)} custom-call(f32[128,128]{1,0:T(8,128)S(1)} %cholesky.272), custom_call_target="Cholesky" | custom-call | tf_op jit(solution)/shard_map/jit(cholesky)/cholesky | solution.py:83
  346.8 9.8 %custom-call.36 = f32[1,128,128]{1,2,0:T(8,128)S(1)} custom-call(f32[1,128,128]{2,1,0:T(8,128)S(1)} %get-tuple-element.39), custom_call_target="InvertDiagBlocksLowerTriangular" | custom-call | tf_op jit(solution)/shard_map/jit(cholesky)/cholesky | solution.py:83
  356.7 0.3 convolution_dynamic-update-slice_fusion.1
  357.0 0.5 convolution_subtract_fusion.9
  357.5 11.9 %cholesky.253 = f32[128,128]{1,0:T(8,128)S(1)} custom-call(f32[128,128]{1,0:T(8,128)S(1)} %convolution_subtract_fusion.9), custom_call_target="Cholesky" | custom-call | tf_op jit(solution)/shard_map/jit(cholesky)/cholesky | solution.py:83
  369.5 0.6 compare_reduce_fusion.2
  371.3 0.6 compare_reduce_fusion.1
  372.7 0.6 compare_reduce_fusion
  374.1 8.1 %while.1 = (s32[]{:T(128)}, f32[512,512]{0,1:T(8,128)S(1)}, s32[4,2]{0,1:T(2,128)S(1)}, f32[4,128,128]{2,1,0:T(8,128)S(1)}, s32[]{:T(128)}) while((s32[]{:T(128)}, f32[512,512]{0,1:T(8,128)S(1)}, s32[4,2]{0,1:T(2,128)S(1)}, f32[4,128,128]{2,1,0:T(8,128)S(1)}, s32[]{:T(128)}) %tuple.34), condition=%wide.while_cond, body=%wide.while_body.sunk | while | flops 2 | bytes 393329 | solution.py:84
  374.2 0.5 fusion.80
  374.7 1.3 dynamic-slice.7
  376.2 0.5 fusion.80
  376.8 1.3 dynamic-slice.7
  378.3 0.5 fusion.80
  378.8 1.3 dynamic-slice.7
  380.3 0.5 fusion.80
  380.8 1.3 dynamic-slice.7
  382.2 39.3 %custom-call.37 = f32[4,128,128]{1,2,0:T(8,128)S(1)} custom-call(f32[4,128,128]{2,1,0:T(8,128)S(1)} %get-tuple-element.13), custom_call_target="InvertDiagBlocksLowerTriangular" | custom-call | tf_op jit(solution)/shard_map/jit(_solve_triangular)/triangular_solve | solution.py:84
  421.6 0.3 fusion.36
  422.0 0.3 convolution_subtract_fusion.5
  422.3 0.3 fusion.53
  422.6 0.4 convolution_subtract_fusion.3
  423.0 0.3 fusion.55
  423.3 0.5 convolution_subtract_fusion.2
  423.8 0.3 fusion.57
  424.2 1.0 copy.26
  425.2 1.0 broadcast_multiply_fusion
  426.8 0.3 convolution_subtract_fusion.7
  427.4 0.4 convolution_subtract_fusion.6
  428.1 0.5 convolution_subtract_fusion.8
  428.6 0.3 fusion.56
  428.9 1.7 convolution_subtract_fusion.1
  (65 shorter events, 3.9 us)
Async XLA Ops:
  7.2 78.2 %all-gather.4.cloned.1.call-start = ((), (), s32[]{:S(2)}) async-start(), calls=%async_computation.2 | async-start | bytes 4456448 | tf_op jit(solution)/shard_map/all_gather | solution.py:21
  7.9 199.6 %reduce-scatter.3.cloned.1.call-start = ((), (), s32[]{:S(2)}) async-start(), calls=%async_computation.3 | async-start | bytes 1892352 | tf_op jit(solution)/shard_map/reduce_scatter | solution.py:44
  85.3 3.4 copy-start.2
  91.6 2.0 copy-start
  97.7 1.9 copy-start.1
  101.9 169.6 %all-gather.6.cloned.1.call-start = ((), (), s32[]{:S(2)}) async-start(), calls=%async_computation.5 | async-start | bytes 1892352 | tf_op jit(solution)/shard_map/all_gather | solution.py:49
  208.9 216.2 %reduce-scatter.5.cloned.1.call-start = ((), (), s32[]{:S(2)}) async-start(), calls=%async_computation.4 | async-start | bytes 12976128 | tf_op jit(solution)/shard_map/reduce_scatter | solution.py:60
  284.6 1.5 copy-start.4
  323.9 97.7 %copy-start.3 = (f32[32,16,256]{2,1,0:T(8,128)S(1)}, f32[32,16,256]{2,1,0:T(8,128)}, u32[]{:S(2)}) copy-start(f32[32,16,256]{2,1,0:T(8,128)} %slice.172) | copy-start | bytes 1572868
Sparse Core Ops, SparseCore 0:
  10.1 75.2 all-gather.3
  102.1 105.3 reduce-scatter.2
  211.2 60.3 all-gather.5
  284.8 125.7 reduce-scatter.4
where the time goes:
time: 444 us; the launch traced here: 437 us
  waiting for transfers between devices  218 us (49%)
  other arithmetic  139 us (31%)
  local copies, waits for them, and re-layouts  41.5 us (9%)
  matrix products  20.7 us (5%)
  between operations  17.7 us (4%)
    reduce_scatter x1, waiting for transfers between devices, shards(): lax.psum_scatter(panel_parts.reshape(par_count * chunk, width), 'par', sc...  105 us
    another operation x14, other arithmetic, shards(): factor = jnp.linalg.cholesky(square_s)  78.7 us
    all_gather x1, waiting for transfers between devices, shards(): gathered = lax.all_gather(jacobian, 'smp', axis=0, tiled=True)  77.4 us
    another operation x3, other arithmetic, shards(): jax.scipy.linalg.solve_triangular(factor, panel_s.T, lower=True)  39.5 us
    all_gather x1, waiting for transfers between devices, shards(): shared = lax.all_gather(reduced, 'par', axis=0, tiled=False)  34.7 us
    reshape x1, local copies, waits for them, and re-layouts, shards(): main_parts.reshape(par_count * main_chunk, width)  13.1 us
    concatenate x1, other arithmetic, shards(): jnp.concatenate([main.reshape(par_count, col_width, width), band.reshape(...  10.5 us
    reshape x1, local copies, waits for them, and re-layouts, shards(): band.reshape(par_count, col_width * PANEL // width, width)  9.33 us
  transfers between devices with their start and end apart: 4, of which 3 were waited for; matrix products, arithmetic and copies ran while one was open for 37% of the time, Pallas kernels for 0%

commit v1 on v0

--- a/solution.py
+++ b/solution.py
@@ -18,7 +18,9 @@
     row_index = lax.axis_index("smp")
     col_index = lax.axis_index("par")
     f32 = jnp.float32
-    gathered = lax.all_gather(jacobian, "smp", axis=0, tiled=True)
+    gathered = jnp.concatenate(
+        lax.all_to_all(jnp.stack([jacobian] * lax.axis_size("smp")), "smp", 0, 0), axis=0
+    )
     widened = gathered.astype(f32)
     col_mean = jnp.sum(widened, axis=0) / sample_total
     centered = (widened - col_mean).astype(jnp.bfloat16)

time: 444 us -> 568 us (1.28)
  waiting for transfers between devices: 218 us -> 317 us
  starting transfers between devices: 0.16 us -> 15.9 us
    all_to_all x0 -> x1, waiting for transfers between devices: none -> 182 us  [shards(): lax.all_to_all(jnp.stack([jacobian] * lax.axis_size('smp')), 'smp', 0, 0)]
    all_gather x1 -> x0, waiting for transfers between devices: 77.4 us -> none  [shards(): gathered = lax.all_gather(jacobian, 'smp', axis=0, tiled=True)]
    all_to_all x0 -> x1, starting transfers between devices: none -> 15.8 us  [shards(): lax.all_to_all(jnp.stack([jacobian] * lax.axis_size('smp')), 'smp', 0, 0)]
  transfers between devices with their start and end apart: 4 -> 4, of which waited for: 3 -> 3; matrix products, arithmetic and copies ran while one was open for 37% -> 29% of each run, Pallas kernels for 0% -> 0%
where the time goes in v1:
time: 568 us; the launch traced here: 560 us
  waiting for transfers between devices  317 us (56%)
  other arithmetic  144 us (25%)
  local copies, waits for them, and re-layouts  44.4 us (8%)
  matrix products  20.7 us (4%)
  between operations  17.7 us (3%)
  starting transfers between devices  15.9 us (3%)
    all_to_all x1, waiting for transfers between devices, shards(): lax.all_to_all(jnp.stack([jacobian] * lax.axis_size('smp')), 'smp', 0, 0)  182 us
    reduce_scatter x1, waiting for transfers between devices, shards(): lax.psum_scatter(panel_parts.reshape(par_count * chunk, width), 'par', sc...  101 us
    another operation x14, other arithmetic, shards(): factor = jnp.linalg.cholesky(square_s)  78.7 us
    another operation x3, other arithmetic, shards(): jax.scipy.linalg.solve_triangular(factor, panel_s.T, lower=True)  39.5 us
    all_gather x1, waiting for transfers between devices, shards(): shared = lax.all_gather(reduced, 'par', axis=0, tiled=False)  34.7 us
    all_to_all x1, starting transfers between devices, shards(): lax.all_to_all(jnp.stack([jacobian] * lax.axis_size('smp')), 'smp', 0, 0)  15.8 us
    reshape x1, local copies, waits for them, and re-layouts, shards(): main_parts.reshape(par_count * main_chunk, width)  13.1 us
  transfers between devices with their start and end apart: 4, of which 3 were waited for; matrix products, arithmetic and copies ran while one was open for 29% of the time, Pallas kernels for 0%

profile of v1, /device:TPU:1, one launch (start us, length us, event | category | flops | bytes accessed | tf_op | source)
XLA Modules:
  0.0 559.8 jit_solution(7416461256797841408)
XLA Ops:
  7.2 3.3 stack.2
  10.5 15.8 %all-to-all-start = ((bf16[16,256,512]{2,1,0:T(8,128)(2,1)}), bf16[16,256,512]{2,1,0:T(8,128)(2,1)}, u32[]{:S(2)}, u32[]{:S(2)}) async-start(bf16[16,256,512]{2,1,0:T(8,128)(2,1)} %stack.2), calls=%async_computation | async-start | bytes 8388608 | tf_op jit(solution)/shard_map/all_to_all | solution.py:22
  26.3 181.7 %all-to-all-done = bf16[16,256,512]{2,1,0:T(8,128)(2,1)} async-done(((bf16[16,256,512]{2,1,0:T(8,128)(2,1)}), bf16[16,256,512]{2,1,0:T(8,128)(2,1)}, u32[]{:S(2)}, u32[]{:S(2)}) %all-to-all-start) | async-done | bytes 4194336 | tf_op jit(solution)/shard_map/all_to_all | solution.py:22
  208.1 2.8 convert_reduce_fusion
  210.9 3.0 fusion
  213.9 2.0 copy-done
  215.8 0.5 fusion.2
  216.5 3.5 fusion.23
  220.0 1.9 copy-done.1
  222.0 5.0 multiply_reduce_fusion
  226.9 0.6 broadcast_in_dim.46
  227.6 1.5 maximum_maximum_fusion
  229.2 100.6 %reduce-scatter.3.cloned.1.call-done = f32[56,256]{1,0:T(8,128)} async-done(((f32[1792,256]{1,0:T(8,128)}), f32[56,256]{1,0:T(8,128)}) %reduce-scatter.3.cloned.1.call-update) | async-done | bytes 57360 | tf_op jit(solution)/shard_map/reduce_scatter | solution.py:46
  329.9 1.4 broadcast_multiply_fusion.1
  331.4 8.0 %fusion.4 = f32[4096,512]{1,0:T(8,128)} fusion(bf16[4096,512]{1,0:T(8,128)(2,1)} %copy-done), kind=kOutput, calls=%fused_computation.32 | convolution fusion | flops 2147483648 | bytes 13107200 | tf_op jit(solution)/shard_map/dot_general | solution.py:32
  339.4 9.3 %reshape.110 = f32[32,256,256]{2,1,0:T(8,128)} reshape(f32[4096,512]{1,0:T(8,128)} %fusion.4) | data formatting | bytes 16777216 | tf_op jit(solution)/shard_map/reshape | solution.py:55
  348.7 10.5 %pad_maximum_fusion = f32[32,384,256]{2,1,0:T(8,128)} fusion(f32[32,256,256]{2,1,0:T(8,128)} %reshape.110, f32[32,128,256]{2,1,0:T(8,128)} %bitcast.79), kind=kLoop, calls=%fused_computation.2 | loop fusion | flops 3145728 | bytes 25165824 | tf_op jit(solution)/shard_map/concatenate | solution.py:52
  359.2 34.7 %all-gather.3.cloned.1.call-done = f32[1792,256]{1,0:T(8,128)} async-done(((f32[56,256]{1,0:T(8,128)}), f32[1792,256]{1,0:T(8,128)}) %all-gather.3.cloned.1.call-update) | async-done | bytes 1835024 | tf_op jit(solution)/shard_map/all_gather | solution.py:51
  393.9 13.1 %copy.43 = f32[12288,256]{0,1:T(8,128)} copy(f32[12288,256]{1,0:T(8,128)} %bitcast.78) | data formatting | bytes 25165824 | tf_op jit(solution)/shard_map/reshape | solution.py:63
  407.1 1.4 copy-done.3
  408.5 0.5 slice.171
  409.0 0.9 slice.172
  410.0 0.3 reshape.114
  410.3 0.3 copy.27
  411.4 0.3 copy.28
  412.0 11.7 %cholesky.103 = f32[128,128]{1,0:T(8,128)S(1)} custom-call(f32[128,128]{1,0:T(8,128)S(1)} %cholesky.263), custom_call_target="Cholesky" | custom-call | tf_op jit(solution)/shard_map/jit(cholesky)/cholesky | solution.py:85
  423.8 9.8 %custom-call.34 = f32[1,128,128]{1,2,0:T(8,128)S(1)} custom-call(f32[1,128,128]{2,1,0:T(8,128)S(1)} %get-tuple-element.47), custom_call_target="InvertDiagBlocksLowerTriangular" | custom-call | tf_op jit(solution)/shard_map/jit(cholesky)/cholesky | solution.py:85
  433.7 0.3 fusion.26
  434.1 0.3 convolution_subtract_fusion
  434.5 11.7 %cholesky.215 = f32[128,128]{1,0:T(8,128)S(1)} custom-call(f32[128,128]{1,0:T(8,128)S(1)} %cholesky.267), custom_call_target="Cholesky" | custom-call | tf_op jit(solution)/shard_map/jit(cholesky)/cholesky | solution.py:85
  446.3 9.9 %custom-call.35 = f32[1,128,128]{1,2,0:T(8,128)S(1)} custom-call(f32[1,128,128]{2,1,0:T(8,128)S(1)} %get-tuple-element.45), custom_call_target="InvertDiagBlocksLowerTriangular" | custom-call | tf_op jit(solution)/shard_map/jit(cholesky)/cholesky | solution.py:85
  456.4 0.3 convolution_dynamic-update-slice_fusion
  456.8 0.6 convolution_subtract_fusion.4
  457.4 11.7 %cholesky.236 = f32[128,128]{1,0:T(8,128)S(1)} custom-call(f32[128,128]{1,0:T(8,128)S(1)} %cholesky.272), custom_call_target="Cholesky" | custom-call | tf_op jit(solution)/shard_map/jit(cholesky)/cholesky | solution.py:85
  469.2 9.8 %custom-call.36 = f32[1,128,128]{1,2,0:T(8,128)S(1)} custom-call(f32[1,128,128]{2,1,0:T(8,128)S(1)} %get-tuple-element.43), custom_call_target="InvertDiagBlocksLowerTriangular" | custom-call | tf_op jit(solution)/shard_map/jit(cholesky)/cholesky | solution.py:85
  479.1 0.3 convolution_dynamic-update-slice_fusion.1
  479.4 0.5 convolution_subtract_fusion.9
  479.8 11.9 %cholesky.253 = f32[128,128]{1,0:T(8,128)S(1)} custom-call(f32[128,128]{1,0:T(8,128)S(1)} %convolution_subtract_fusion.9), custom_call_target="Cholesky" | custom-call | tf_op jit(solution)/shard_map/jit(cholesky)/cholesky | solution.py:85
  491.9 0.6 compare_reduce_fusion.2
  493.7 0.6 compare_reduce_fusion.1
  495.0 0.6 compare_reduce_fusion
  496.5 8.1 %while.1 = (s32[]{:T(128)}, f32[512,512]{0,1:T(8,128)S(1)}, s32[4,2]{0,1:T(2,128)S(1)}, f32[4,128,128]{2,1,0:T(8,128)S(1)}, s32[]{:T(128)}) while((s32[]{:T(128)}, f32[512,512]{0,1:T(8,128)S(1)}, s32[4,2]{0,1:T(2,128)S(1)}, f32[4,128,128]{2,1,0:T(8,128)S(1)}, s32[]{:T(128)}) %tuple.35), condition=%wide.while_cond, body=%wide.while_body.sunk | while | flops 2 | bytes 393329 | solution.py:86
  496.6 0.5 fusion.79
  497.1 1.3 dynamic-slice.7
  498.6 0.5 fusion.79
  499.1 1.3 dynamic-slice.7
  500.6 0.5 fusion.79
  501.2 1.3 dynamic-slice.7
  502.7 0.5 fusion.79
  503.2 1.3 dynamic-slice.7
  504.6 39.3 %custom-call.37 = f32[4,128,128]{1,2,0:T(8,128)S(1)} custom-call(f32[4,128,128]{2,1,0:T(8,128)S(1)} %get-tuple-element.13), custom_call_target="InvertDiagBlocksLowerTriangular" | custom-call | tf_op jit(solution)/shard_map/jit(_solve_triangular)/triangular_solve | solution.py:86
  544.0 0.3 fusion.36
  544.4 0.3 convolution_subtract_fusion.5
  544.7 0.3 fusion.53
  545.0 0.4 convolution_subtract_fusion.3
  545.4 0.3 fusion.55
  545.7 0.5 convolution_subtract_fusion.2
  546.2 0.3 fusion.57
  546.6 1.0 copy.40
  547.6 1.0 broadcast_multiply_fusion
  549.3 0.3 convolution_subtract_fusion.7
  549.9 0.4 convolution_subtract_fusion.6
  550.6 0.5 convolution_subtract_fusion.8
  551.4 1.7 convolution_subtract_fusion.1
  (65 shorter events, 4.2 us)
Async XLA Ops:
  10.5 197.6 %all-to-all-start = ((bf16[16,256,512]{2,1,0:T(8,128)(2,1)}), bf16[16,256,512]{2,1,0:T(8,128)(2,1)}, u32[]{:S(2)}, u32[]{:S(2)}) async-start(bf16[16,256,512]{2,1,0:T(8,128)(2,1)} %stack.2), calls=%async_computation | async-start | bytes 8388608 | tf_op jit(solution)/shard_map/all_to_all | solution.py:22
  26.3 303.6 %reduce-scatter.3.cloned.1.call-start = ((), (), s32[]{:S(2)}) async-start(), calls=%async_computation.3 | async-start | bytes 1892352 | tf_op jit(solution)/shard_map/reduce_scatter | solution.py:46
  213.9 2.0 copy-start
  220.0 1.9 copy-start.1
  229.2 164.7 %all-gather.3.cloned.1.call-start = ((), (), s32[]{:S(2)}) async-start(), calls=%async_computation.5 | async-start | bytes 1892352 | tf_op jit(solution)/shard_map/all_gather | solution.py:51
  331.3 216.2 %reduce-scatter.5.cloned.1.call-start = ((), (), s32[]{:S(2)}) async-start(), calls=%async_computation.4 | async-start | bytes 12976128 | tf_op jit(solution)/shard_map/reduce_scatter | solution.py:62
  407.0 1.5 copy-start.3
  446.3 97.7 %copy-start.2 = (f32[32,16,256]{2,1,0:T(8,128)S(1)}, f32[32,16,256]{2,1,0:T(8,128)}, u32[]{:S(2)}) copy-start(f32[32,16,256]{2,1,0:T(8,128)} %slice.172) | copy-start | bytes 1572868
Sparse Core Ops, SparseCore 0:
  229.3 100.4 reduce-scatter.2
  333.6 60.3 all-gather.2
  407.1 125.6 reduce-scatter.4
